TPU v7x, 256 devices: a whole 4x4x8 slice. The times are simulated.
256 devices in a mesh: tm: 128 (over z, y_lo, x, core), net: 2 (over y_hi).
Axes of the slice: x: 4, y: 4 (y_hi: 2, y_lo: 2; y = y_hi * 2 + y_lo), z: 8, core: 2. Of those that a mesh axis runs over, the one named last changes fastest.
Arguments:
- direction_nodal: float32 [1, 128, 2, 8192], P(None, 'tm', None, 'net'), may hold values from -27 to 27
- direction_capacity: float32 [1, 128, 65536], P(None, 'tm', 'net'), may hold values from -27 to 27
- residual_nodal: float32 [1, 128, 2, 8192], P(None, 'tm', None, 'net'), may hold values from -27 to 27
- residual_capacity: float32 [1, 128, 65536], P(None, 'tm', 'net'), may hold values from -27 to 27
- scale_flow: float32 [128, 12288], P('tm', 'net'), may hold values from 0.25 to 4
- scale_dispatch: float32 [128, 65536], P('tm', 'net'), may hold values from 0.25 to 4
- scale_storage: float32 [128, 2, 8192], P('tm', None, 'net'), may hold values from 0.25 to 4
- scale_capacity: float32 [65536], P('net'), may hold values from 0.02 to 0.3
- availability: float32 [128, 65536], P('tm', 'net'), may hold values from 0.05 to 1
- retention: float32 [8192], P('net'), may hold values from 0.5 to 1
- line_anchor: int32 [96], P('net'), may hold values from 0 to 63
- line_target: int32 [96], P('net'), may hold values from 0 to 63
- anchor_rows: int32 [12288], P('net'), may hold values from 0 to 127
- target_rows: int32 [12288], P('net'), may hold values from 0 to 127
- column_block: int32 [512], P('net'), may hold values from 0 to 63
- column_rows: int32 [65536], P('net'), may hold values from 0 to 127
Outputs:
- updated_nodal: float32 [1, 128, 2, 8192], P(None, 'tm', None, 'net')
- updated_capacity: float32 [1, 128, 65536], P(None, 'tm', 'net')
All inputs are finite; a program needn't handle non-finite values.
Results may differ from a plain program's by a relative error of at most 0.00002.
Values sent between devices are 32-bit elements; how exact they have to be, the bound alone decides.
No kernel may reach another device: no remote copies, remote signals or barrier semaphores. Data moves between devices by JAX's collectives and lax.ppermute only.
A program may use at most 64 MiB of HBM per device.

v0:
```python
import jax
import jax.numpy as jnp
from jax import lax
from jax.sharding import PartitionSpec as P

BLOCK = 128
DAMPING = 0.5


def passed_along(value, axis, steps):
    count = lax.axis_size(axis)
    pairs = [(source, (source + steps) % count) for source in range(count)]
    return lax.ppermute(value, axis, pairs)


def body(
    direction_nodal,
    direction_capacity,
    residual_nodal,
    residual_capacity,
    scale_flow,
    scale_dispatch,
    scale_storage,
    scale_capacity,
    availability,
    retention,
    line_anchor,
    line_target,
    anchor_rows,
    target_rows,
    column_block,
    column_rows,
):
    anchor = jnp.repeat(line_anchor, BLOCK) * BLOCK + anchor_rows
    target = jnp.repeat(line_target, BLOCK) * BLOCK + target_rows
    column_bus = jnp.repeat(column_block, BLOCK) * BLOCK + column_rows
    balance = direction_nodal[:, :, 0, :]
    storage = direction_nodal[:, :, 1, :]
    network = lax.all_gather(balance, "net", axis=2, tiled=True)
    next_first = passed_along(storage, "tm", -1)
    storage_next = jnp.concatenate([storage[:, 1:, :], next_first], axis=1)
    flow_value = jnp.take(network, anchor, axis=2) - jnp.take(network, target, axis=2)
    dispatch_value = jnp.take(network, column_bus, axis=2) + direction_capacity
    partial_sums = -jnp.sum(availability[None] * direction_capacity, axis=1)
    level_value = storage - retention * storage_next
    charge_value = balance - storage
    flow_scaled = scale_flow[None] * flow_value
    dispatch_scaled = scale_dispatch[None] * dispatch_value
    level_scaled = scale_storage[None, :, 0, :] * level_value
    charge_scaled = scale_storage[None, :, 1, :] * charge_value
    capacity_value = lax.psum(partial_sums, "tm")
    capacity_scaled = scale_capacity[None] * capacity_value
    squares_local = jnp.sum(residual_nodal * residual_nodal, axis=(1, 2, 3)) + jnp.sum(
        residual_capacity * residual_capacity, axis=(1, 2)
    )
    bus_terms = jnp.zeros(network.shape, jnp.float32).at[:, :, anchor].add(flow_scaled)
    bus_terms = (
        bus_terms.at[:, :, target].add(-flow_scaled).at[:, :, column_bus].add(dispatch_scaled)
    )
    own_terms = lax.psum_scatter(bus_terms, "net", scatter_dimension=2, tiled=True)
    image_balance = own_terms + charge_scaled + DAMPING * balance
    behind = passed_along(level_scaled, "tm", 1)
    level_before = jnp.concatenate([behind, level_scaled[:, :-1, :]], axis=1)
    image_storage = level_scaled - retention * level_before - charge_scaled + DAMPING * storage
    image_limit = (
        dispatch_scaled
        - availability[None] * capacity_scaled[:, None, :]
        + DAMPING * direction_capacity
    )
    image_nodal = jnp.stack([image_balance, image_storage], axis=2)
    curvature_local = jnp.sum(direction_nodal * image_nodal, axis=(1, 2, 3)) + jnp.sum(
        direction_capacity * image_limit, axis=(1, 2)
    )
    squares, curvature = lax.psum((squares_local, curvature_local), ("tm", "net"))
    step_size = squares / curvature
    updated_nodal = residual_nodal - step_size[:, None, None, None] * image_nodal
    updated_capacity = residual_capacity - step_size[:, None, None] * image_limit
    return (updated_nodal, updated_capacity)


def solution(mesh):
    in_specs = (
        P(None, "tm", None, "net"),
        P(None, "tm", "net"),
        P(None, "tm", None, "net"),
        P(None, "tm", "net"),
        P("tm", "net"),
        P("tm", "net"),
        P("tm", None, "net"),
        P("net"),
        P("tm", "net"),
        P("net"),
        P("net"),
        P("net"),
        P("net"),
        P("net"),
        P("net"),
        P("net"),
    )
    out_specs = (P(None, "tm", None, "net"), P(None, "tm", "net"))
    return jax.shard_map(body, mesh=mesh, in_specs=in_specs, out_specs=out_specs, check_vma=False)
```

profile of v0, /device:TPU:1, one launch (start us, length us, event | category | flops | bytes accessed | tf_op | source)
XLA Modules:
  0.0 1337.2 jit_solution(10901547301141026485)
XLA Ops:
  7.2 0.0 all-reduce.3.cloned.1.call-start
  7.2 1.8 fusion.3
  9.0 0.0 all-reduce.3.cloned.1.call-update
  9.0 0.0 reduce-scatter.4.cloned.1.call-start
  9.1 0.9 fusion.11
  9.9 3.3 collective-permute-start
  13.3 4.8 all-gather
  18.0 0.7 broadcast_multiply_fusion.1
  18.7 0.7 broadcast_multiply_fusion.2
  19.3 0.8 broadcast_clamp_fusion.1
  20.2 34.3 %gather_fusion.2 = f32[6144]{0:T(1024)S(1)} fusion(f32[8192]{0:T(1024)S(1)} %bitcast.85, s32[6144]{0:T(1024)S(1)} %get-tuple-element.12), kind=kCustom, calls=%fused_computation.1.clone | custom fusion | bytes 73728 | tf_op jit(solution)/shard_map/jit(_take)/gather | solution.py:42
  54.5 0.1 broadcast_clamp_fusion.2
  54.6 34.3 %gather_fusion.1 = f32[6144]{0:T(1024)S(1)} fusion(f32[8192]{0:T(1024)S(1)} %bitcast.86, s32[6144]{0:T(1024)S(1)} %get-tuple-element.14), kind=kCustom, calls=%fused_computation.clone | custom fusion | bytes 73728 | tf_op jit(solution)/shard_map/jit(_take)/gather | solution.py:42
  88.9 0.1 broadcast_clamp_fusion
  89.0 180.5 %gather_fusion = f32[32768]{0:T(1024)S(1)} fusion(f32[8192]{0:T(1024)S(1)} %bitcast.87, s32[32768]{0:T(1024)S(1)} %get-tuple-element.8), kind=kCustom, calls=%fused_computation.2 | custom fusion | bytes 393216 | tf_op jit(solution)/shard_map/jit(_take)/gather | solution.py:43
  269.7 0.1 fusion.10
  269.7 0.9 multiply_reduce_fusion.1
  270.6 42.8 %scatter_custom_fusion = f32[8192]{0:T(1024)S(1)} fusion(s32[6144]{0:T(1024)S(1)} %get-tuple-element.15, f32[6144]{0:T(1024)S(1)} %bitcast.99, f32[]{:T(128)} %constant.15.clone.1), kind=kCustom, calls=%fused_computation.36 | custom fusion | flops 6144 | bytes 32772 | tf_op jit(solution)/shard_map/scatter-add | solution.py:56
  313.5 42.9 %scatter_fusion = f32[8192]{0:T(1024)S(1)} fusion(f32[8192]{0:T(1024)S(1)} %scatter_custom_fusion, s32[6144]{0:T(1024)S(1)} %get-tuple-element.13, f32[6144]{0:T(1024)S(1)} %bitcast.94), kind=kCustom, calls=%fused_computation.4 | custom fusion | flops 6144 | bytes 98304 | tf_op jit(solution)/shard_map/scatter-add | solution.py:58
  356.5 0.6 collective-permute-start.1
  357.1 593.0 %all-reduce.3.cloned.1.call-done = f32[1,32768]{1,0:T(1,128)} async-done(((f32[1,32768]{1,0:T(1,128)}), f32[1,32768]{1,0:T(1,128)}) %all-reduce.3.cloned.1.call-update) | async-done | bytes 131088 | tf_op jit(solution)/shard_map/psum | solution.py:51
  950.2 1.9 multiply_reduce_fusion
  952.1 225.9 %scatter_fusion.1 = f32[8192]{0:T(1024)S(1)} fusion(f32[8192]{0:T(1024)S(1)} %scatter_fusion, s32[32768]{0:T(1024)S(1)} %get-tuple-element.9, f32[32768]{0:T(1024)S(1)} %bitcast.91), kind=kCustom, calls=%fused_computation.5 | custom fusion | flops 32768 | bytes 524288 | tf_op jit(solution)/shard_map/scatter-add | solution.py:58
  1178.1 6.4 copy.18
  1184.5 0.6 multiply_reduce_fusion.3
  1186.3 57.5 %reduce-scatter.4.cloned.1.call-done = f32[4096,1]{1,0:T(8,128)} async-done(((f32[8192,1]{1,0:T(8,128)}), f32[4096,1]{1,0:T(8,128)}) %reduce-scatter.4.cloned.1.call-update) | async-done | bytes 16400
  1243.8 4.4 copy.19
  1248.3 0.1 fusion.5
  1248.4 0.7 multiply_reduce_fusion.2
  1250.4 77.2 %all-reduce = (f32[1]{0:T(128)}, f32[1]{0:T(128)}) all-reduce(f32[1]{0:T(128)} %bitcast.2, f32[1]{0:T(128)} %bitcast.31), channel_id=1, replica_groups=mesh['tm'=128,'net'=2] {'tm','net'}, use_global_device_ids=true, to_apply=%region_2.3 | all-reduce | flops 2 | bytes 16 | tf_op jit(solution)/shard_map/psum | solution.py:74
  1328.9 0.7 multiply_subtract_fusion.1
  1329.6 0.8 multiply_subtract_fusion
  (34 shorter events, 0.2 us)
Async XLA Ops:
  7.2 943.0 %all-reduce.3.cloned.1.call-start = ((), (), s32[]{:S(2)}) async-start(), calls=%async_computation.1 | async-start | bytes 262144 | tf_op jit(solution)/shard_map/psum | solution.py:51
  9.0 1234.8 %reduce-scatter.4.cloned.1.call-start = ((), (), s32[]{:S(2)}) async-start(), calls=%async_computation.2 | async-start | bytes 6291456
  9.9 346.5 %collective-permute-start = (f32[1,1,4096]{2,1,0:T(1,128)S(1)}, f32[1,1,4096]{2,1,0:T(1,128)S(1)}, u32[]{:S(2)}, u32[]{:S(2)}) collective-permute-start(f32[1,1,4096]{2,1,0:T(1,128)S(1)} %get-tuple-element.19), channel_id=1, source_target_pairs={{0,254},{2,0},{4,2},{6,4},{8,6},{10,8},{12,10},{14,12},{16,14},{18... | collective-permute-start | bytes 49160 | tf_op jit(solution)/shard_map/ppermute | solution.py:13
  20.2 34.3 %copy-start.10 = (s32[6144]{0:T(1024)S(1)}, s32[6144]{0:T(1024)}, u32[]{:S(2)}) copy-start(s32[6144]{0:T(1024)} %param.30) | copy-start | bytes 73732
  54.6 34.3 %copy-start.12 = (s32[256]{0:T(256)S(1)}, s32[256]{0:T(256)}, u32[]{:S(2)}) copy-start(s32[256]{0:T(256)} %param.32) | copy-start | bytes 3076
  54.6 34.3 %copy-start.4 = (s32[32768]{0:T(1024)S(1)}, s32[32768]{0:T(1024)}, u32[]{:S(2)}) copy-start(s32[32768]{0:T(1024)} %param.33) | copy-start | bytes 393220
  89.0 180.6 %copy-start.11 = (f32[1,6144]{1,0:T(1,128)S(1)}, f32[1,6144]{1,0:T(1,128)}, u32[]{:S(2)}) copy-start(f32[1,6144]{1,0:T(1,128)} %param.22) | copy-start | bytes 73732
  89.0 180.7 %copy-start = (f32[1,1,32768]{2,1,0:T(1,128)S(1)}, f32[1,1,32768]{2,1,0:T(1,128)}, u32[]{:S(2)}) copy-start(f32[1,1,32768]{2,1,0:T(1,128)} %param.21) | copy-start | bytes 393220
  313.4 43.0 %copy-start.3 = (f32[1,1,2,4096]{3,2,1,0:T(2,128)S(1)}, f32[1,1,2,4096]{3,2,1,0:T(2,128)}, u32[]{:S(2)}) copy-start(f32[1,1,2,4096]{3,2,1,0:T(2,128)} %param.18) | copy-start | bytes 98308
  313.5 43.0 %copy-start.8 = (f32[4096]{0:T(1024)S(1)}, f32[4096]{0:T(1024)}, u32[]{:S(2)}) copy-start(f32[4096]{0:T(1024)} %param.27) | copy-start | bytes 49156
  313.5 43.0 %copy-start.9 = (f32[1,2,4096]{2,1,0:T(2,128)S(1)}, f32[1,2,4096]{2,1,0:T(2,128)}, u32[]{:S(2)}) copy-start(f32[1,2,4096]{2,1,0:T(2,128)} %param.24) | copy-start | bytes 98308
  313.5 636.7 %copy-start.1 = (f32[1,1,32768]{2,1,0:T(1,128)S(1)}, f32[1,1,32768]{2,1,0:T(1,128)}, u32[]{:S(2)}) copy-start(f32[1,1,32768]{2,1,0:T(1,128)} %param.19) | copy-start | bytes 393220
  313.5 636.7 %copy-start.2 = (f32[1,32768]{1,0:T(1,128)S(1)}, f32[1,32768]{1,0:T(1,128)}, u32[]{:S(2)}) copy-start(f32[1,32768]{1,0:T(1,128)} %param.26) | copy-start | bytes 393220
  313.5 636.7 %copy-start.6 = (f32[32768]{0:T(1024)S(1)}, f32[32768]{0:T(1024)}, u32[]{:S(2)}) copy-start(f32[32768]{0:T(1024)} %param.25) | copy-start | bytes 393220
  313.5 636.7 %copy-start.7 = (f32[1,32768]{1,0:T(1,128)S(1)}, f32[1,32768]{1,0:T(1,128)}, u32[]{:S(2)}) copy-start(f32[1,32768]{1,0:T(1,128)} %param.23) | copy-start | bytes 393220
  356.5 891.7 %collective-permute-start.1 = (f32[1,1,4096]{2,1,0:T(1,128)S(1)}, f32[1,1,4096]{2,1,0:T(1,128)S(1)}, u32[]{:S(2)}, u32[]{:S(2)}) collective-permute-start(f32[1,1,4096]{2,1,0:T(1,128)S(1)} %subtract_multiply_fusion), channel_id=1, source_target_pairs={{0,2},{2,4},{4,6},{6,8},{8,10},{10,12},{12,14},{14,16},{16,18},{18... | collective-permute-start | bytes 49160 | tf_op jit(solution)/shard_map/ppermute | solution.py:13
  1178.1 6.4 copy-start.5
Sparse Core Ops, SparseCore 0:
  11.2 938.9 all-reduce.2
  1184.6 59.2 reduce-scatter.3
where the time goes:
time: 1340 us
  waiting for transfers between devices  651 us (49%)
  other arithmetic  322 us (24%)
  local copies, waits for them, and re-layouts  261 us (19%)
  blocking collectives  81.9 us (6%)
  between operations  18.3 us (1%)
    psum x1, waiting for transfers between devices, body(): capacity_value = lax.psum(partial_sums, 'tm')  593 us
    scatter-add x2, other arithmetic, body(): bus_terms.at[:, :, target].add(-flow_scaled).at[:, :, column_bus]  269 us
    gather x1, local copies, waits for them, and re-layouts, body(): dispatch_value = jnp.take(network, column_bus, axis=2) + direction_capacity  181 us
    psum x1, blocking collectives, body(): lax.psum((squares_local, curvature_local), ('tm', 'net'))  77.2 us
    unnamed x3, waiting for transfers between devices  57.5 us
    scatter-add x1, other arithmetic, body(): jnp.zeros(network.shape, jnp.float32).at[:, :, anchor].add(flow_scaled)  42.8 us
    gather x1, local copies, waits for them, and re-layouts, body(): jnp.take(network, target, axis=2)  34.3 us
    gather x1, local copies, waits for them, and re-layouts, body(): jnp.take(network, anchor, axis=2) - jnp.take(network, target, axis=2)  34.3 us
  transfers between devices with their start and end apart: 4, of which 2 were waited for; matrix products, arithmetic and copies ran while one was open for 43% of the time, Pallas kernels for 0%

commit v1 on v0

--- a/solution.py
+++ b/solution.py
@@ -48,7 +48,7 @@
     dispatch_scaled = scale_dispatch[None] * dispatch_value
     level_scaled = scale_storage[None, :, 0, :] * level_value
     charge_scaled = scale_storage[None, :, 1, :] * charge_value
-    capacity_value = lax.psum(partial_sums, "tm")
+    capacity_value = jnp.sum(lax.all_gather(partial_sums, "tm"), axis=0)
     capacity_scaled = scale_capacity[None] * capacity_value
     squares_local = jnp.sum(residual_nodal * residual_nodal, axis=(1, 2, 3)) + jnp.sum(
         residual_capacity * residual_capacity, axis=(1, 2)

time: 1340 us -> 762 us (0.57)
  waiting for transfers between devices: 651 us -> 64.1 us
    psum x1 -> x0, waiting for transfers between devices: 593 us -> none  [body(): capacity_value = lax.psum(partial_sums, 'tm')]
  transfers between devices with their start and end apart: 4 -> 4, of which waited for: 2 -> 1; matrix products, arithmetic and copies ran while one was open for 43% -> 77% of each run, Pallas kernels for 0% -> 0%
where the time goes in v1:
time: 762 us
  other arithmetic  332 us (44%)
  local copies, waits for them, and re-layouts  261 us (34%)
  blocking collectives  81.9 us (11%)
  waiting for transfers between devices  64.1 us (8%)
  between operations  18.3 us (2%)
    scatter-add x2, other arithmetic, body(): bus_terms.at[:, :, target].add(-flow_scaled).at[:, :, column_bus]  269 us
    gather x1, local copies, waits for them, and re-layouts, body(): dispatch_value = jnp.take(network, column_bus, axis=2) + direction_capacity  181 us
    psum x1, blocking collectives, body(): lax.psum((squares_local, curvature_local), ('tm', 'net'))  77.1 us
    unnamed x3, waiting for transfers between devices  64.1 us
    scatter-add x1, other arithmetic, body(): jnp.zeros(network.shape, jnp.float32).at[:, :, anchor].add(flow_scaled)  42.8 us
    gather x1, local copies, waits for them, and re-layouts, body(): jnp.take(network, target, axis=2)  34.3 us
    gather x1, local copies, waits for them, and re-layouts, body(): jnp.take(network, anchor, axis=2) - jnp.take(network, target, axis=2)  34.3 us
  transfers between devices with their start and end apart: 4, of which 1 were waited for; matrix products, arithmetic and copies ran while one was open for 77% of the time, Pallas kernels for 0%

profile of v1, /device:TPU:1, one launch (start us, length us, event | category | flops | bytes accessed | tf_op | source)
XLA Modules:
  0.0 761.6 jit_solution(17253483734441213888)
XLA Ops:
  7.2 0.0 all-gather.3.cloned.1.call-start
  7.2 1.8 fusion
  9.0 0.0 all-gather.3.cloned.1.call-update
  9.0 0.0 reduce-scatter.4.cloned.1.call-start
  9.1 0.9 fusion.7
  9.9 3.3 collective-permute-start
  13.3 4.8 all-gather
  18.0 0.7 broadcast_multiply_fusion.1
  18.7 0.8 broadcast_clamp_fusion.1
  19.5 34.3 %gather_fusion.2 = f32[6144]{0:T(1024)S(1)} fusion(f32[8192]{0:T(1024)S(1)} %bitcast.73, s32[6144]{0:T(1024)S(1)} %get-tuple-element.11), kind=kCustom, calls=%fused_computation.1.clone | custom fusion | bytes 73728 | tf_op jit(solution)/shard_map/jit(_take)/gather | solution.py:42
  53.8 0.1 broadcast_clamp_fusion.2
  54.0 34.3 %gather_fusion.1 = f32[6144]{0:T(1024)S(1)} fusion(f32[8192]{0:T(1024)S(1)} %bitcast.74, s32[6144]{0:T(1024)S(1)} %get-tuple-element.13), kind=kCustom, calls=%fused_computation.clone | custom fusion | bytes 73728 | tf_op jit(solution)/shard_map/jit(_take)/gather | solution.py:42
  88.3 0.1 broadcast_clamp_fusion
  88.4 180.5 %gather_fusion = f32[32768]{0:T(1024)S(1)} fusion(f32[8192]{0:T(1024)S(1)} %bitcast.75, s32[32768]{0:T(1024)S(1)} %get-tuple-element.7), kind=kCustom, calls=%fused_computation.2 | custom fusion | bytes 393216 | tf_op jit(solution)/shard_map/jit(_take)/gather | solution.py:43
  269.0 0.1 fusion.6
  269.1 0.9 multiply_reduce_fusion.1
  270.0 42.8 %scatter_custom_fusion = f32[8192]{0:T(1024)S(1)} fusion(s32[6144]{0:T(1024)S(1)} %get-tuple-element.14, f32[6144]{0:T(1024)S(1)} %bitcast.89, f32[]{:T(128)} %constant.15.clone.1), kind=kCustom, calls=%fused_computation.34 | custom fusion | flops 6144 | bytes 32772 | tf_op jit(solution)/shard_map/scatter-add | solution.py:56
  312.9 42.9 %scatter_fusion = f32[8192]{0:T(1024)S(1)} fusion(f32[8192]{0:T(1024)S(1)} %scatter_custom_fusion, s32[6144]{0:T(1024)S(1)} %get-tuple-element.12, f32[6144]{0:T(1024)S(1)} %bitcast.84), kind=kCustom, calls=%fused_computation.4 | custom fusion | flops 6144 | bytes 98304 | tf_op jit(solution)/shard_map/scatter-add | solution.py:58
  356.0 0.6 collective-permute-start.1
  356.6 12.5 %reduce_sum.52 = f32[32768]{0:T(1024)S(1)} reduce(f32[128,1,32768]{2,1,0:T(1,128)} %all-gather.3.cloned.1.call-done, f32[]{:T(128)} %constant.15.clone.1), dimensions={0,1}, to_apply=%region_8.10 | reduce | flops 4161536 | bytes 16908292 | tf_op jit(solution)/shard_map/reduce_sum | solution.py:51
  369.1 0.9 multiply_reduce_fusion
  370.0 225.9 %scatter_fusion.1 = f32[8192]{0:T(1024)S(1)} fusion(f32[8192]{0:T(1024)S(1)} %scatter_fusion, s32[32768]{0:T(1024)S(1)} %get-tuple-element.8, f32[32768]{0:T(1024)S(1)} %bitcast.79), kind=kCustom, calls=%fused_computation.5 | custom fusion | flops 32768 | bytes 524288 | tf_op jit(solution)/shard_map/scatter-add | solution.py:58
  596.0 6.4 copy.18
  602.3 0.0 reduce-scatter.4.cloned.1.call-update
  602.4 0.6 multiply_reduce_fusion.3
  604.3 64.0 %reduce-scatter.4.cloned.1.call-done = f32[4096,1]{1,0:T(8,128)} async-done(((f32[8192,1]{1,0:T(8,128)}), f32[4096,1]{1,0:T(8,128)}) %reduce-scatter.4.cloned.1.call-update) | async-done | bytes 16400
  668.4 4.4 copy.19
  672.8 0.1 fusion.2
  672.9 0.6 multiply_reduce_fusion.2
  674.7 77.1 %all-reduce = (f32[1]{0:T(128)}, f32[1]{0:T(128)}) all-reduce(f32[1]{0:T(128)} %bitcast.2, f32[1]{0:T(128)} %bitcast.30), channel_id=1, replica_groups=mesh['tm'=128,'net'=2] {'tm','net'}, use_global_device_ids=true, to_apply=%region_2.3 | all-reduce | flops 2 | bytes 16 | tf_op jit(solution)/shard_map/psum | solution.py:74
  753.2 0.9 multiply_subtract_fusion
  754.1 0.7 multiply_subtract_fusion.1
  (38 shorter events, 0.2 us)
Async XLA Ops:
  7.2 349.4 %all-gather.3.cloned.1.call-start = ((), (), s32[]{:S(2)}) async-start(), calls=%async_computation.1 | async-start | bytes 16908288 | tf_op jit(solution)/shard_map/all_gather | solution.py:51
  9.0 659.3 %reduce-scatter.4.cloned.1.call-start = ((), (), s32[]{:S(2)}) async-start(), calls=%async_computation.2 | async-start | bytes 6291456
  9.9 345.9 %collective-permute-start = (f32[1,1,4096]{2,1,0:T(1,128)S(1)}, f32[1,1,4096]{2,1,0:T(1,128)S(1)}, u32[]{:S(2)}, u32[]{:S(2)}) collective-permute-start(f32[1,1,4096]{2,1,0:T(1,128)S(1)} %get-tuple-element.18), channel_id=1, source_target_pairs={{0,254},{2,0},{4,2},{6,4},{8,6},{10,8},{12,10},{14,12},{16,14},{18... | collective-permute-start | bytes 49160 | tf_op jit(solution)/shard_map/ppermute | solution.py:13
  19.5 34.3 %copy-start.13 = (s32[48]{0:T(128)S(1)}, s32[48]{0:T(128)}, u32[]{:S(2)}) copy-start(s32[48]{0:T(128)} %param.28) | copy-start | bytes 580
  19.5 34.3 %copy-start.10 = (s32[6144]{0:T(1024)S(1)}, s32[6144]{0:T(1024)}, u32[]{:S(2)}) copy-start(s32[6144]{0:T(1024)} %param.30) | copy-start | bytes 73732
  53.9 34.3 %copy-start.12 = (s32[256]{0:T(256)S(1)}, s32[256]{0:T(256)}, u32[]{:S(2)}) copy-start(s32[256]{0:T(256)} %param.32) | copy-start | bytes 3076
  53.9 34.3 %copy-start.4 = (s32[32768]{0:T(1024)S(1)}, s32[32768]{0:T(1024)}, u32[]{:S(2)}) copy-start(s32[32768]{0:T(1024)} %param.33) | copy-start | bytes 393220
  88.4 180.6 %copy-start.11 = (f32[1,6144]{1,0:T(1,128)S(1)}, f32[1,6144]{1,0:T(1,128)}, u32[]{:S(2)}) copy-start(f32[1,6144]{1,0:T(1,128)} %param.22) | copy-start | bytes 73732
  88.4 180.7 %copy-start.2 = (f32[1,1,32768]{2,1,0:T(1,128)S(1)}, f32[1,1,32768]{2,1,0:T(1,128)}, u32[]{:S(2)}) copy-start(f32[1,1,32768]{2,1,0:T(1,128)} %param.21) | copy-start | bytes 393220
  312.9 43.0 %copy-start.3 = (f32[1,1,2,4096]{3,2,1,0:T(2,128)S(1)}, f32[1,1,2,4096]{3,2,1,0:T(2,128)}, u32[]{:S(2)}) copy-start(f32[1,1,2,4096]{3,2,1,0:T(2,128)} %param.18) | copy-start | bytes 98308
  312.9 43.0 %copy-start.8 = (f32[4096]{0:T(1024)S(1)}, f32[4096]{0:T(1024)}, u32[]{:S(2)}) copy-start(f32[4096]{0:T(1024)} %param.27) | copy-start | bytes 49156
  312.9 43.0 %copy-start.9 = (f32[1,2,4096]{2,1,0:T(2,128)S(1)}, f32[1,2,4096]{2,1,0:T(2,128)}, u32[]{:S(2)}) copy-start(f32[1,2,4096]{2,1,0:T(2,128)} %param.24) | copy-start | bytes 98308
  355.9 13.1 %copy-start.1 = (f32[1,32768]{1,0:T(1,128)S(1)}, f32[1,32768]{1,0:T(1,128)}, u32[]{:S(2)}) copy-start(f32[1,32768]{1,0:T(1,128)} %param.26) | copy-start | bytes 393220
  355.9 13.1 %copy-start.6 = (f32[32768]{0:T(1024)S(1)}, f32[32768]{0:T(1024)}, u32[]{:S(2)}) copy-start(f32[32768]{0:T(1024)} %param.25) | copy-start | bytes 393220
  356.0 13.1 %copy-start = (f32[1,1,32768]{2,1,0:T(1,128)S(1)}, f32[1,1,32768]{2,1,0:T(1,128)}, u32[]{:S(2)}) copy-start(f32[1,1,32768]{2,1,0:T(1,128)} %param.19) | copy-start | bytes 393220
  356.0 13.1 %copy-start.7 = (f32[1,32768]{1,0:T(1,128)S(1)}, f32[1,32768]{1,0:T(1,128)}, u32[]{:S(2)}) copy-start(f32[1,32768]{1,0:T(1,128)} %param.23) | copy-start | bytes 393220
  356.0 316.8 %collective-permute-start.1 = (f32[1,1,4096]{2,1,0:T(1,128)S(1)}, f32[1,1,4096]{2,1,0:T(1,128)S(1)}, u32[]{:S(2)}, u32[]{:S(2)}) collective-permute-start(f32[1,1,4096]{2,1,0:T(1,128)S(1)} %subtract_multiply_fusion), channel_id=1, source_target_pairs={{0,2},{2,4},{4,6},{6,8},{8,10},{10,12},{12,14},{14,16},{16,18},{18... | collective-permute-start | bytes 49160 | tf_op jit(solution)/shard_map/ppermute | solution.py:13
  595.9 6.4 copy-start.5
Sparse Core Ops, SparseCore 0:
  10.4 232.9 all-gather.2
  602.5 65.8 reduce-scatter.3
